TPU v7x, 32 devices: a whole 2x2x4 slice. The times are simulated.
32 devices in a mesh: shard: 4 (over z), rep: 8 (over y, x, core).
Axes of the slice: x: 2, y: 2, z: 4, core: 2. Of those that a mesh axis runs over, the one named last changes fastest.
Arguments:
- grads: bfloat16 [1, 8192, 28672], P(None, 'shard', 'rep'), may hold values from -81 to 81
- seeds: int32 [1], replicated, may hold values from 0 to 999999
Outputs:
- projected: bfloat16 [512, 1, 28672], P('shard', None, 'rep')
All inputs are finite; a program needn't handle non-finite values.
Results may differ from a plain program's by a relative error of at most 0.0056.
Values may be sent and summed in bfloat16 or wider, within the bound.
No kernel may reach another device: no remote copies, remote signals or barrier semaphores. Data moves between devices by JAX's collectives and lax.ppermute only.
A program may use at most 128 MiB of HBM per device.

v0:
```python
import jax
import jax.numpy as jnp
from jax import lax
from jax.sharding import PartitionSpec as P

RANK = 512
mix_first = 668265263
mix_second = -2048144789
mix_third = -1028477387


def sketch_table(seeds, first_row, count, rank):
    rows = first_row + lax.iota(jnp.int32, count)
    columns = lax.iota(jnp.int32, rank)
    counter = rows[:, None] * jnp.int32(rank) + columns[None, :]
    hashed = jnp.bitwise_xor(counter[None, :, :], (seeds * jnp.int32(mix_first))[:, None, None])
    hashed = hashed * jnp.int32(mix_second)
    hashed = jnp.bitwise_xor(hashed, lax.shift_right_logical(hashed, jnp.int32(15)))
    hashed = hashed * jnp.int32(mix_third)
    hashed = jnp.bitwise_xor(hashed, lax.shift_right_logical(hashed, jnp.int32(13)))
    unit = lax.shift_right_logical(hashed, jnp.int32(8)).astype(jnp.float32) * (1.0 / 16777216.0)
    return (2.0 * unit - 1.0).astype(jnp.bfloat16)


def body(grads, seeds):
    mats, depth, width = grads.shape
    col0 = lax.axis_index("rep") * width
    outs = []
    for m in range(mats):
        table = sketch_table(seeds[m : m + 1], col0, width, RANK)[0]
        g = grads[m]
        partial = jnp.dot(g, table, preferred_element_type=jnp.float32)
        sketch_rows = lax.psum(partial, "rep")
        local_gram = jnp.dot(
            sketch_rows.T,
            sketch_rows,
            precision=lax.Precision.HIGHEST,
            preferred_element_type=jnp.float32,
        )
        gram = lax.psum(local_gram, "shard")
        factor = jnp.linalg.cholesky(gram)
        basis_rows = lax.linalg.triangular_solve(
            factor, sketch_rows, left_side=False, lower=True, transpose_a=True
        ).astype(jnp.bfloat16)
        partial_sum = jnp.dot(basis_rows.T, g, preferred_element_type=jnp.float32)
        outs.append(partial_sum)
    partial_sum = jnp.stack(outs, axis=1).astype(jnp.bfloat16)
    return lax.psum_scatter(partial_sum, "shard", scatter_dimension=0, tiled=True)


def solution(mesh):
    return jax.shard_map(
        body,
        mesh=mesh,
        in_specs=(P(None, "shard", "rep"), P()),
        out_specs=P("shard", None, "rep"),
        check_vma=False,
    )
```

profile of v0, /device:TPU:0, one launch (start us, length us, event | category | flops | bytes accessed | tf_op | source)
XLA Modules:
  0.0 411.4 jit_solution(13956208684615322948)
XLA Ops:
  7.2 16.7 %fusion.27 = f32[2048,512]{0,1:T(8,128)} fusion(bf16[1,2048,3584]{2,1,0:T(8,128)(2,1)} %param.2, s32[]{:T(128)} %bitcast, s32[3584]{0:T(1024)S(1)} %add_multiply_fusion), kind=kOutput, calls=%fused_computation.26 | convolution fusion | flops 7540047872 | bytes 18888708 | tf_op jit(solution)/shard_map/dot_general | solution.py:32
  24.3 83.4 %all-reduce.4.cloned.1.call-done = f32[2048,512]{0,1:T(8,128)} async-done(((f32[2048,512]{0,1:T(8,128)}), f32[2048,512]{0,1:T(8,128)}) %all-reduce.4.cloned.1.call-update) | async-done | bytes 4194320 | tf_op jit(solution)/shard_map/psum | solution.py:33
  107.6 10.2 %fusion.84 = f32[512,512]{0,1:T(8,128)} fusion(f32[2048,512]{0,1:T(8,128)} %all-reduce.4.cloned.1.call-done), kind=kOutput, calls=%fused_computation.111 | convolution fusion | flops 6442450944 | bytes 5242880 | tf_op jit(solution)/shard_map/dot_general | solution.py:34
  118.0 52.0 %all-reduce.6.cloned.1.call-done = f32[512,512]{0,1:T(8,128)} async-done(((f32[512,512]{0,1:T(8,128)}), f32[512,512]{0,1:T(8,128)}) %all-reduce.6.cloned.1.call-update) | async-done | bytes 1048592 | tf_op jit(solution)/shard_map/psum | solution.py:40
  170.0 1.6 copy.6
  171.6 1.4 fusion.53
  173.0 11.7 %cholesky.104 = f32[128,128]{1,0:T(8,128)S(1)} custom-call(f32[128,128]{1,0:T(8,128)S(1)} %cholesky.266), custom_call_target="Cholesky" | custom-call | tf_op jit(solution)/shard_map/jit(cholesky)/cholesky | solution.py:41
  184.8 9.8 %custom-call.30 = f32[1,128,128]{1,2,0:T(8,128)S(1)} custom-call(f32[1,128,128]{2,1,0:T(8,128)S(1)} %get-tuple-element.32), custom_call_target="InvertDiagBlocksLowerTriangular" | custom-call | tf_op jit(solution)/shard_map/jit(cholesky)/cholesky | solution.py:41
  195.4 11.7 %cholesky.217 = f32[128,128]{1,0:T(8,128)S(1)} custom-call(f32[128,128]{1,0:T(8,128)S(1)} %cholesky.270), custom_call_target="Cholesky" | custom-call | tf_op jit(solution)/shard_map/jit(cholesky)/cholesky | solution.py:41
  207.2 18.5 %custom-call.31 = f32[1,128,128]{1,2,0:T(8,128)S(1)} custom-call(f32[1,128,128]{2,1,0:T(8,128)S(1)} %get-tuple-element.29), custom_call_target="InvertDiagBlocksLowerTriangular" | custom-call | tf_op jit(solution)/shard_map/jit(cholesky)/cholesky | solution.py:41
  226.3 11.7 %cholesky.238 = f32[128,128]{1,0:T(8,128)S(1)} custom-call(f32[128,128]{1,0:T(8,128)S(1)} %cholesky.275), custom_call_target="Cholesky" | custom-call | tf_op jit(solution)/shard_map/jit(cholesky)/cholesky | solution.py:41
  238.1 0.7 compare_reduce_fusion.1
  238.7 9.8 %custom-call.32 = f32[1,128,128]{1,2,0:T(8,128)S(1)} custom-call(f32[1,128,128]{2,1,0:T(8,128)S(1)} %get-tuple-element.26), custom_call_target="InvertDiagBlocksLowerTriangular" | custom-call | tf_op jit(solution)/shard_map/jit(cholesky)/cholesky | solution.py:41
  249.2 11.7 %cholesky.255 = f32[128,128]{1,0:T(8,128)S(1)} custom-call(f32[128,128]{1,0:T(8,128)S(1)} %convolution_subtract_fusion.4), custom_call_target="Cholesky" | custom-call | tf_op jit(solution)/shard_map/jit(cholesky)/cholesky | solution.py:41
  260.9 0.7 compare_reduce_fusion
  261.6 0.7 compare_reduce_fusion.2
  265.1 7.8 %while.1 = (s32[]{:T(128)}, f32[512,512]{1,0:T(8,128)S(1)}, s32[4,2]{0,1:T(2,128)S(1)}, f32[4,128,128]{2,1,0:T(8,128)S(1)}, s32[]{:T(128)}) while((s32[]{:T(128)}, f32[512,512]{1,0:T(8,128)S(1)}, s32[4,2]{0,1:T(2,128)S(1)}, f32[4,128,128]{2,1,0:T(8,128)S(1)}, s32[]{:T(128)}) %tuple.30), condition=%wide.while_cond, body=%wide.while_body.sunk | while | flops 2 | bytes 131189 | solution.py:42
  265.8 1.3 bitcast_dynamic-update-slice_fusion.2
  267.2 0.5 fusion.93
  267.7 1.3 bitcast_dynamic-update-slice_fusion.2
  269.7 1.3 bitcast_dynamic-update-slice_fusion.2
  271.6 1.3 bitcast_dynamic-update-slice_fusion.2
  273.0 39.3 %custom-call.33 = f32[4,128,128]{1,2,0:T(8,128)S(1)} custom-call(f32[4,128,128]{2,1,0:T(8,128)S(1)} %get-tuple-element.12), custom_call_target="InvertDiagBlocksLowerTriangular" | custom-call | tf_op jit(solution)/shard_map/triangular_solve | solution.py:42
  312.3 2.5 fusion.83
  314.8 2.3 convolution_subtract_fusion.1
  317.1 1.1 fusion.82
  318.2 1.3 convolution_subtract_fusion
  319.5 1.1 fusion.81
  320.6 2.2 fusion.38
  322.8 1.1 convolution_convert_fusion
  323.9 12.6 %fusion.13 = bf16[512,1,3584]{2,0,1:T(8,128)(2,1)} fusion(bf16[1,2048,3584]{2,1,0:T(8,128)(2,1)} %param.2, bf16[2048,128]{0,1:T(8,128)(2,1)S(1)} %convolution_convert_fusion, bf16[2048,128]{0,1:T(8,128)(2,1)S(1)} %get-tuple-element.35, bf16[2048,128]{0,1:T(8,128)(2,1)S(1)} %get-tuple-element.37, bf16[2048,128]{0,1:T(8,128)(2,1)S(1)} %get-tuple-element.39), kind=kOutput, calls=%fused_computation.15 | convolution fusion | flops 7526416384 | bytes 20447232 | tf_op jit(solution)/shard_map/dot_general | solution.py:45
  336.5 68.0 %reduce-scatter.2.cloned.1.call-done = bf16[128,1,3584]{2,0,1:T(8,128)(2,1)} async-done(((bf16[512,1,3584]{2,0,1:T(8,128)(2,1)}), bf16[128,1,3584]{2,0,1:T(8,128)(2,1)}) %reduce-scatter.2.cloned.1.call-update) | async-done | bytes 917520 | tf_op jit(solution)/shard_map/reduce_scatter | solution.py:48
  (34 shorter events, 4.8 us)
Async XLA Ops:
  6.5 101.1 %all-reduce.4.cloned.1.call-start = ((), (), s32[]{:S(2)}) async-start(), calls=%async_computation.1 | async-start | bytes 8388608 | tf_op jit(solution)/shard_map/psum | solution.py:33
  23.9 146.1 %all-reduce.6.cloned.1.call-start = ((), (), s32[]{:S(2)}) async-start(), calls=%async_computation.2 | async-start | bytes 2097152 | tf_op jit(solution)/shard_map/psum | solution.py:40
  117.9 286.6 %reduce-scatter.2.cloned.1.call-start = ((), (), s32[]{:S(2)}) async-start(), calls=%async_computation.3 | async-start | bytes 4587520 | tf_op jit(solution)/shard_map/reduce_scatter | solution.py:48
  312.3 5.9 %copy-start = (f32[2048,512]{0,1:T(8,128)S(1)}, f32[2048,512]{0,1:T(8,128)}, u32[]{:S(2)}) copy-start(f32[2048,512]{0,1:T(8,128)} %all-reduce.4.cloned.1.call-done) | copy-start | bytes 12582916
Sparse Core Ops, SparseCore 0:
  24.1 83.5 all-reduce.3
  118.0 51.9 all-reduce.5
  336.6 67.8 reduce-scatter.1
where the time goes:
time: 419 us; the launch traced here: 411 us
  waiting for transfers between devices  203 us (48%)
  other arithmetic  128 us (31%)
  matrix products  52.9 us (13%)
  between operations  16.9 us (4%)
  local copies, waits for them, and re-layouts  9.44 us (2%)
    another operation x14, other arithmetic, body(): factor = jnp.linalg.cholesky(gram)  87.2 us
    psum x1, waiting for transfers between devices, body(): sketch_rows = lax.psum(partial, 'rep')  83.4 us
    reduce_scatter x1, waiting for transfers between devices, body(): lax.psum_scatter(partial_sum, 'shard', scatter_dimension=0, tiled=True)  68 us
    psum x1, waiting for transfers between devices, body(): gram = lax.psum(local_gram, 'shard')  52 us
    another operation x3, other arithmetic, body(): lax.linalg.triangular_solve(factor, sketch_rows, left_side=False, lower=T...  39.7 us
    dot_general x1, matrix products, body(): partial = jnp.dot(g, table, preferred_element_type=jnp.float32)  16.7 us
    dot_general x1, matrix products, body(): partial_sum = jnp.dot(basis_rows.T, g, preferred_element_type=jnp.float32)  12.6 us
    another operation x7, matrix products, body(): lax.linalg.triangular_solve(factor, sketch_rows, left_side=False, lower=T...  11.5 us
  transfers between devices with their start and end apart: 3, of which 3 were waited for; matrix products, arithmetic and copies ran while one was open for 0% of the time, Pallas kernels for 0%

commit v1 on v0

--- a/solution.py
+++ b/solution.py
@@ -30,7 +30,7 @@
         table = sketch_table(seeds[m : m + 1], col0, width, RANK)[0]
         g = grads[m]
         partial = jnp.dot(g, table, preferred_element_type=jnp.float32)
-        sketch_rows = lax.psum(partial, "rep")
+        sketch_rows = jnp.sum(lax.all_gather(partial, "rep"), axis=0)
         local_gram = jnp.dot(
             sketch_rows.T,
             sketch_rows,

time: 419 us -> 556 us (1.33)
  waiting for transfers between devices: 203 us -> 277 us
  local copies, waits for them, and re-layouts: 9.44 us -> 55.2 us
  matrix products: 52.9 us -> 64.2 us
  other arithmetic: 128 us -> 134 us
    all_gather x0 -> x1, waiting for transfers between devices: none -> 163 us  [body(): sketch_rows = jnp.sum(lax.all_gather(partial, 'rep'), axis=0)]
    psum x1 -> x0, waiting for transfers between devices: 83.4 us -> none  [body(): sketch_rows = lax.psum(partial, 'rep')]
    unnamed x2 -> x8, local copies, waits for them, and re-layouts: 0.01 us -> 36.7 us
    reduce_sum x0 -> x1, other arithmetic: none -> 12.7 us  [body(): sketch_rows = jnp.sum(lax.all_gather(partial, 'rep'), axis=0)]
    another operation x14, other arithmetic: 87.2 us -> 78.8 us  [body(): factor = jnp.linalg.cholesky(gram)]
    another operation x7, matrix products: 11.5 us -> 19.3 us  [body(): lax.linalg.triangular_solve(factor, sketch_rows, left_side=False, lower=T...]
    psum x1, waiting for transfers between devices: 52 us -> 45.3 us  [body(): gram = lax.psum(local_gram, 'shard')]
    another operation x12, local copies, waits for them, and re-layouts: 7.74 us -> 13.8 us
  transfers between devices with their start and end apart: 3 -> 3, of which waited for: 3 -> 3; matrix products, arithmetic and copies ran while one was open for 0% -> 1% of each run, Pallas kernels for 0% -> 0%
where the time goes in v1:
time: 556 us; the launch traced here: 548 us
  waiting for transfers between devices  277 us (50%)
  other arithmetic  134 us (24%)
  matrix products  64.2 us (12%)
  local copies, waits for them, and re-layouts  55.2 us (10%)
  between operations  16.9 us (3%)
    all_gather x1, waiting for transfers between devices, body(): sketch_rows = jnp.sum(lax.all_gather(partial, 'rep'), axis=0)  163 us
    another operation x14, other arithmetic, body(): factor = jnp.linalg.cholesky(gram)  78.8 us
    reduce_scatter x1, waiting for transfers between devices, body(): lax.psum_scatter(partial_sum, 'shard', scatter_dimension=0, tiled=True)  68 us
    psum x1, waiting for transfers between devices, body(): gram = lax.psum(local_gram, 'shard')  45.3 us
    another operation x3, other arithmetic, body(): lax.linalg.triangular_solve(factor, sketch_rows, left_side=False, lower=T...  41.3 us
    unnamed x8, local copies, waits for them, and re-layouts  36.7 us
    another operation x7, matrix products, body(): lax.linalg.triangular_solve(factor, sketch_rows, left_side=False, lower=T...  19.3 us
    dot_general x1, matrix products, body(): partial = jnp.dot(g, table, preferred_element_type=jnp.float32)  16.8 us
  transfers between devices with their start and end apart: 3, of which 3 were waited for; matrix products, arithmetic and copies ran while one was open for 1% of the time, Pallas kernels for 0%

profile of v1, /device:TPU:0, one launch (start us, length us, event | category | flops | bytes accessed | tf_op | source)
XLA Modules:
  0.0 547.8 jit_solution(15405139574117030837)
XLA Ops:
  7.2 16.8 %fusion.27 = f32[2048,512]{0,1:T(8,128)} fusion(bf16[1,2048,3584]{2,1,0:T(8,128)(2,1)} %param.2, s32[]{:T(128)} %bitcast, s32[3584]{0:T(1024)S(1)} %add_multiply_fusion), kind=kOutput, calls=%fused_computation.27 | convolution fusion | flops 7540047872 | bytes 18888708 | tf_op jit(solution)/shard_map/dot_general | solution.py:32
  24.3 163.3 %all-gather.3.cloned.1.call-done = f32[16384,512]{0,1:T(8,128)} async-done(((f32[2048,512]{0,1:T(8,128)}), f32[16384,512]{0,1:T(8,128)}) %all-gather.3.cloned.1.call-update) | async-done | bytes 33554448 | tf_op jit(solution)/shard_map/all_gather | solution.py:33
  187.6 32.5 %copy.16 = f32[64,8,8,2048]{3,2,1,0:T(8,128)S(1)} copy(f32[64,8,8,2048]{3,1,2,0:T(8,128)} %bitcast.82) | data formatting | bytes 67108864
  220.1 12.7 %bitcast_reduce_fusion = f32[2048,512]{0,1:T(8,128)} fusion(f32[64,8,8,2048]{3,2,1,0:T(8,128)S(1)} %copy.16), kind=kLoop, calls=%fused_computation.2 | loop fusion | flops 7340032 | bytes 37748736 | tf_op jit(solution)/shard_map/reduce_sum | solution.py:33
  232.7 10.2 %fusion.85 = f32[512,512]{0,1:T(8,128)} fusion(f32[2048,512]{0,1:T(8,128)} %bitcast_reduce_fusion), kind=kOutput, calls=%fused_computation.113 | convolution fusion | flops 6442450944 | bytes 5242880 | tf_op jit(solution)/shard_map/dot_general | solution.py:34
  243.5 3.1 fusion.81
  246.6 1.5 copy.13
  248.1 1.3 copy.14
  249.8 45.3 %all-reduce.3.cloned.1.call-done = f32[512,512]{0,1:T(8,128)} async-done(((f32[512,512]{0,1:T(8,128)}), f32[512,512]{0,1:T(8,128)}) %all-reduce.3.cloned.1.call-update) | async-done | bytes 1048592 | tf_op jit(solution)/shard_map/psum | solution.py:40
  295.1 1.6 copy.8
  296.6 1.4 fusion.53
  299.1 11.7 %cholesky.104 = f32[128,128]{1,0:T(8,128)S(1)} custom-call(f32[128,128]{1,0:T(8,128)S(1)} %cholesky.266), custom_call_target="Cholesky" | custom-call | tf_op jit(solution)/shard_map/jit(cholesky)/cholesky | solution.py:41
  310.8 9.8 %custom-call.30 = f32[1,128,128]{1,2,0:T(8,128)S(1)} custom-call(f32[1,128,128]{2,1,0:T(8,128)S(1)} %get-tuple-element.35), custom_call_target="InvertDiagBlocksLowerTriangular" | custom-call | tf_op jit(solution)/shard_map/jit(cholesky)/cholesky | solution.py:41
  322.0 1.3 convolution_subtract_fusion.2
  323.3 11.7 %cholesky.217 = f32[128,128]{1,0:T(8,128)S(1)} custom-call(f32[128,128]{1,0:T(8,128)S(1)} %cholesky.270), custom_call_target="Cholesky" | custom-call | tf_op jit(solution)/shard_map/jit(cholesky)/cholesky | solution.py:41
  335.1 10.0 %custom-call.31 = f32[1,128,128]{1,2,0:T(8,128)S(1)} custom-call(f32[1,128,128]{2,1,0:T(8,128)S(1)} %get-tuple-element.32), custom_call_target="InvertDiagBlocksLowerTriangular" | custom-call | tf_op jit(solution)/shard_map/jit(cholesky)/cholesky | solution.py:41
  345.3 1.3 convolution_subtract_fusion.3
  346.6 11.7 %cholesky.238 = f32[128,128]{1,0:T(8,128)S(1)} custom-call(f32[128,128]{1,0:T(8,128)S(1)} %cholesky.275), custom_call_target="Cholesky" | custom-call | tf_op jit(solution)/shard_map/jit(cholesky)/cholesky | solution.py:41
  359.0 9.8 %custom-call.32 = f32[1,128,128]{1,2,0:T(8,128)S(1)} custom-call(f32[1,128,128]{2,1,0:T(8,128)S(1)} %get-tuple-element.29), custom_call_target="InvertDiagBlocksLowerTriangular" | custom-call | tf_op jit(solution)/shard_map/jit(cholesky)/cholesky | solution.py:41
  370.2 11.9 %cholesky.255 = f32[128,128]{1,0:T(8,128)S(1)} custom-call(f32[128,128]{1,0:T(8,128)S(1)} %convolution_subtract_fusion.4), custom_call_target="Cholesky" | custom-call | tf_op jit(solution)/shard_map/jit(cholesky)/cholesky | solution.py:41
  387.2 13.8 %while.1 = (s32[]{:T(128)}, f32[512,512]{1,0:T(8,128)}, s32[4,2]{0,1:T(2,128)S(1)}, f32[4,128,128]{2,1,0:T(8,128)}, s32[]{:T(128)}) while((s32[]{:T(128)}, f32[512,512]{1,0:T(8,128)}, s32[4,2]{0,1:T(2,128)S(1)}, f32[4,128,128]{2,1,0:T(8,128)}, s32[]{:T(128)}) %tuple.32), condition=%wide.while_cond, body=%wide.while_body.sunk | while | flops 2 | bytes 132705 | solution.py:42
  387.8 2.8 bitcast_dynamic-update-slice_fusion.2
  391.3 2.8 bitcast_dynamic-update-slice_fusion.2
  394.7 2.8 bitcast_dynamic-update-slice_fusion.2
  398.2 2.8 bitcast_dynamic-update-slice_fusion.2
  400.9 40.1 %custom-call.33 = f32[4,128,128]{1,2,0:T(8,128)S(1)} custom-call(f32[4,128,128]{2,1,0:T(8,128)} %get-tuple-element.12), custom_call_target="InvertDiagBlocksLowerTriangular" | custom-call | tf_op jit(solution)/shard_map/triangular_solve | solution.py:42
  441.1 2.4 fusion.84
  443.5 2.7 convolution_subtract_fusion.1
  447.2 4.5 convolution_subtract_fusion
  452.8 6.5 %fusion.38 = f32[2048,128]{1,0:T(8,128)S(1)} fusion(f32[2048,128]{1,0:T(8,128)S(1)} %copy.15, f32[2048,128]{0,1:T(8,128)S(1)} %get-tuple-element.39, f32[2048,128]{0,1:T(8,128)S(1)} %get-tuple-element.41, f32[2048,128]{0,1:T(8,128)S(1)} %get-tuple-element.43, f32[512,512]{1,0:T(8,128)} %get-tuple-element.101), kind=kOutput, calls=%fused_computation.34 | convolution fusion | flops 1209794560 | bytes 5439488 | tf_op jit(solution)/shard_map/triangular_solve | solution.py:42
  460.4 12.4 %fusion.13 = bf16[512,1,3584]{2,0,1:T(8,128)(2,1)} fusion(bf16[1,2048,3584]{2,1,0:T(8,128)(2,1)} %param.2, bf16[2048,128]{0,1:T(8,128)(2,1)S(1)} %convolution_convert_fusion, bf16[2048,128]{0,1:T(8,128)(2,1)S(1)} %get-tuple-element.38, bf16[2048,128]{0,1:T(8,128)(2,1)S(1)} %get-tuple-element.40, bf16[2048,128]{0,1:T(8,128)(2,1)S(1)} %get-tuple-element.42), kind=kOutput, calls=%fused_computation.16 | convolution fusion | flops 7526416384 | bytes 20447232 | tf_op jit(solution)/shard_map/dot_general | solution.py:45
  472.9 68.0 %reduce-scatter.2.cloned.1.call-done = bf16[128,1,3584]{2,0,1:T(8,128)(2,1)} async-done(((bf16[512,1,3584]{2,0,1:T(8,128)(2,1)}), bf16[128,1,3584]{2,0,1:T(8,128)(2,1)}) %reduce-scatter.2.cloned.1.call-update) | async-done | bytes 917520 | tf_op jit(solution)/shard_map/reduce_scatter | solution.py:48
  (42 shorter events, 14.2 us)
Async XLA Ops:
  6.5 181.0 %all-gather.3.cloned.1.call-start = ((), (), s32[]{:S(2)}) async-start(), calls=%async_computation.3 | async-start | bytes 37748736 | tf_op jit(solution)/shard_map/all_gather | solution.py:33
  24.0 271.0 %all-reduce.3.cloned.1.call-start = ((), (), s32[]{:S(2)}) async-start(), calls=%async_computation.1 | async-start | bytes 2097152 | tf_op jit(solution)/shard_map/psum | solution.py:40
  243.0 297.8 %reduce-scatter.2.cloned.1.call-start = ((), (), s32[]{:S(2)}) async-start(), calls=%async_computation.2 | async-start | bytes 4587520 | tf_op jit(solution)/shard_map/reduce_scatter | solution.py:48
  298.1 1.0 copy-start.1
  441.1 6.2 %copy-start = (f32[2048,128]{1,0:T(8,128)S(1)}, f32[2048,128]{1,0:T(8,128)}, u32[]{:S(2)}) copy-start(f32[2048,128]{1,0:T(8,128)} %copy.14) | copy-start | bytes 3145732
Sparse Core Ops, SparseCore 0:
  24.1 163.3 all-gather.2
  243.1 51.8 all-reduce.2
  473.0 67.8 reduce-scatter.1
